TPU v7x, 128 devices: a whole 4x4x4 slice. The times are simulated.
128 devices in a mesh: seq: 32 (over y, x, core), mp: 4 (over z).
Axes of the slice: x: 4, y: 4, z: 4, core: 2. Of those that a mesh axis runs over, the one named last changes fastest.
Arguments:
- states: bfloat16 [4, 16, 2048], P(None, None, 'mp'), may hold values from -4 to 4
- query_weight: bfloat16 [2048, 2048], P('seq', 'mp'), may hold values from -5 to 5
- key_weight: bfloat16 [2048, 2048], P('seq', 'mp'), may hold values from -5 to 5
- value_weight: bfloat16 [2048, 2048], P('seq', 'mp'), may hold values from -5 to 5
- output_weight: bfloat16 [2048, 2048], P('seq', 'mp'), may hold values from -5 to 5
- gate_weight: bfloat16 [2048, 8192], P('seq', 'mp'), may hold values from -5 to 5
- up_weight: bfloat16 [2048, 8192], P('seq', 'mp'), may hold values from -5 to 5
- down_weight: bfloat16 [8192, 2048], P('seq', 'mp'), may hold values from -5 to 5
- query_gain: float32 [2048], P('mp'), may hold values from 0.5 to 2
- key_gain: float32 [2048], P('mp'), may hold values from 0.5 to 2
- attention_gain: float32 [2048], P('mp'), may hold values from 0.1 to 1.9
- feedforward_gain: float32 [2048], P('mp'), may hold values from 0.1 to 1.9
- key_cache: bfloat16 [512, 256, 2048], P('seq', None, 'mp'), may hold values from -500 to 500
- value_cache: bfloat16 [512, 256, 2048], P('seq', None, 'mp'), may hold values from -6 to 6
- lengths: int32 [16], replicated, may hold values from 1 to 32768, as said below
- page_owner: int32 [512], P('seq'), may hold values from -1 to 15, as said below
- page_index: int32 [512], P('seq'), may hold values from 0 to 127, as said below
Outputs:
- decoded: bfloat16 [4, 16, 2048], P(None, None, 'mp')
Inputs may be any that keep to these rules, and one draw needn't show every extreme that they name: Request r owns exactly ceil(lengths[r] / 256) pages. `page_owner`: on each device of seq the used pages come before the unused ones. `page_index`: the pages of one request carry the numbers 0, 1, 2 and so on, once each; unused pages carry 0.
All inputs are finite; a program needn't handle non-finite values.
Results may differ from a plain program's by a relative error of at most 0.015.
Values may be sent and summed in bfloat16 or wider, within the bound.
No kernel may reach another device: no remote copies, remote signals or barrier semaphores. Data moves between devices by JAX's collectives and lax.ppermute only.
A program may use at most 64 MiB of HBM per device.

v0:
```python
import jax
import jax.numpy as jnp
from jax import lax
from jax.sharding import PartitionSpec as P

D = 2048
HD = 128
R = 16
STEPS = 4
PAGE = 256
epsilon = 1e-06
rope_base = 500000.0
very_low = -1e30
exact_mode = lax.Precision.HIGHEST
pages_per_block = 4


def combined_all(value, axis, join):
    pieces = jax.tree.map(lambda part: lax.all_gather(part, axis), value)
    head = jax.tree.map(lambda part: part[0], pieces)
    tail = jax.tree.map(lambda part: part[1:], pieces)
    subtotal, _ = lax.scan(lambda subtotal, piece: (join(subtotal, piece), None), head, tail)
    return subtotal


def rotary(values, positions):
    half_width = HD // 2
    frequencies = rope_base ** (-2.0 * jnp.arange(half_width, dtype=jnp.float32) / HD)
    angles = positions.astype(jnp.float32)[:, None] * frequencies[None, :]
    cosine = jnp.cos(angles)[:, None, :]
    sine_part = jnp.sin(angles)[:, None, :]
    first_half = values[..., :half_width]
    second_half = values[..., half_width:]
    return jnp.concatenate(
        [
            first_half * cosine - second_half * sine_part,
            second_half * cosine + first_half * sine_part,
        ],
        axis=-1,
    )


def seq_columns(token_rows, width):
    gathered = lax.all_gather(token_rows, "mp", axis=1, tiled=True)
    return lax.dynamic_slice_in_dim(gathered, lax.axis_index("seq") * width, width, 1)


def seq_total(partial_value):
    return lax.psum(partial_value, "seq")


def feature_sums(squares):
    return lax.psum(squares, "mp")


def inverse_rms(square_total):
    return lax.rsqrt(square_total / D + epsilon)[:, None]


def combine_parts(earlier, later_part):
    highest = jnp.maximum(earlier[0], later_part[0])
    first_scale = jnp.exp(earlier[0] - highest)
    second_scale = jnp.exp(later_part[0] - highest)
    return (
        highest,
        earlier[1] * first_scale + later_part[1] * second_scale,
        earlier[2] * first_scale[..., None] + later_part[2] * second_scale[..., None],
    )


def local(
    states,
    query_weight,
    key_weight,
    value_weight,
    output_weight,
    gate_weight,
    up_weight,
    down_weight,
    query_gain,
    key_gain,
    attention_gain,
    feedforward_gain,
    key_cache,
    value_cache,
    lengths,
    page_owner,
    page_index,
):
    local_width = query_weight.shape[1]
    local_heads = local_width // HD
    requests = jnp.arange(R, dtype=jnp.int32)
    score_scale = HD ** (-0.5)
    outputs = []
    key_list = []
    value_list = []
    for step_index in range(STEPS):
        token_rows = states[step_index]
        positions = lengths + step_index
        attention_row_count = token_rows.shape[0]
        attention_sliced = seq_columns(token_rows, query_weight.shape[0])
        partial_value = jnp.concatenate(
            [
                jnp.dot(attention_sliced, query_weight, preferred_element_type=jnp.float32),
                jnp.dot(attention_sliced, key_weight, preferred_element_type=jnp.float32),
                jnp.dot(attention_sliced, value_weight, preferred_element_type=jnp.float32),
            ],
            axis=1,
        )
        summed = seq_total(partial_value)
        query_raw = summed[:, :local_width]
        key_raw = summed[:, local_width : 2 * local_width]
        value_raw = summed[:, 2 * local_width :]
        squares = feature_sums(
            jnp.stack(
                [jnp.sum(query_raw * query_raw, axis=1), jnp.sum(key_raw * key_raw, axis=1)], axis=1
            )
        )
        attention_queries = query_raw * inverse_rms(squares[:, 0]) * query_gain
        attention_new_keys = key_raw * inverse_rms(squares[:, 1]) * key_gain
        attention_queries = rotary(
            attention_queries.reshape(attention_row_count, local_heads, HD), positions
        ).astype(jnp.bfloat16)
        attention_new_keys = rotary(
            attention_new_keys.reshape(attention_row_count, local_heads, HD), positions
        ).astype(jnp.bfloat16)
        attention_new_values = value_raw.astype(jnp.bfloat16).reshape(
            attention_row_count, local_heads, HD
        )
        key_list.append(attention_new_keys[None])
        value_list.append(attention_new_values[None])
        cache_queries = attention_queries[None]
        steps_here = cache_queries.shape[0]

        def fold_block(block_index, carried):
            maxima, totals, running = carried
            first_page = block_index * pages_per_block
            key_block = lax.dynamic_slice_in_dim(key_cache, first_page, pages_per_block, 0).reshape(
                pages_per_block, PAGE, local_heads, HD
            )
            value_block = lax.dynamic_slice_in_dim(
                value_cache, first_page, pages_per_block, 0
            ).reshape(pages_per_block, PAGE, local_heads, HD)
            owners = lax.dynamic_slice_in_dim(page_owner, first_page, pages_per_block, 0)
            indices = lax.dynamic_slice_in_dim(page_index, first_page, pages_per_block, 0)
            matches = owners[:, None] == requests[None, :]
            onehot = matches.astype(jnp.float32)
            picked = jnp.take(cache_queries, jnp.maximum(owners, 0), axis=1)
            scores = (
                jnp.einsum("sghd,gthd->sgth", picked, key_block, preferred_element_type=jnp.float32)
                * score_scale
            )
            page_lengths = jnp.sum(jnp.where(matches, lengths[None, :], 0), axis=1)
            token_spots = indices[:, None] * PAGE + jnp.arange(PAGE, dtype=jnp.int32)[None, :]
            validity = (token_spots < page_lengths[:, None])[None, :, :, None]
            masked = jnp.where(validity, scores, very_low)
            page_top = jnp.max(masked, axis=2)
            request_top = jnp.max(
                jnp.where(matches.T[None, :, :, None], page_top[:, None, :, :], very_low), axis=2
            )
            highest = jnp.maximum(maxima, request_top)
            page_ref = jnp.take(highest, jnp.maximum(owners, 0), axis=1)
            weights = jnp.where(validity, jnp.exp(masked - page_ref[:, :, None, :]), 0.0)
            page_total = jnp.sum(weights, axis=2)
            page_sum = jnp.einsum(
                "sgth,gthd->sghd",
                weights.astype(jnp.bfloat16),
                value_block,
                preferred_element_type=jnp.float32,
            )
            factor = jnp.exp(maxima - highest)
            totals = totals * factor + jnp.einsum(
                "gr,sgh->srh", onehot, page_total, precision=exact_mode
            )
            running = running * factor[..., None] + jnp.einsum(
                "gr,sghd->srhd", onehot, page_sum, precision=exact_mode
            )
            return (highest, totals, running)

        block_count = page_owner.shape[0] // pages_per_block
        initial = (
            jnp.full((steps_here, R, local_heads), very_low, jnp.float32),
            jnp.zeros((steps_here, R, local_heads), jnp.float32),
            jnp.zeros((steps_here, R, local_heads, HD), jnp.float32),
        )
        maxima, totals, running = lax.fori_loop(0, block_count, fold_block, initial)
        merged_parts = combined_all((maxima, totals, running), "seq", combine_parts)
        finish_queries = attention_queries[None]
        finish_new_keys = jnp.concatenate(key_list, axis=0)
        finish_maxima, finish_totals, finish_running = merged_parts
        finish_steps_here = finish_queries.shape[0]
        known = finish_new_keys.shape[0]
        fresh_scores = (
            jnp.einsum(
                "srhd,trhd->srht",
                finish_queries,
                finish_new_keys,
                preferred_element_type=jnp.float32,
            )
            * score_scale
        )
        allowed = (
            jnp.arange(known)[None, :] <= step_index + jnp.arange(finish_steps_here)[:, None]
        )[:, None, None, :]
        fresh_scores = jnp.where(allowed, fresh_scores, very_low)
        finish_highest = jnp.maximum(finish_maxima, jnp.max(fresh_scores, axis=-1))
        fresh_weights = jnp.where(allowed, jnp.exp(fresh_scores - finish_highest[..., None]), 0.0)
        finish_factor = jnp.exp(finish_maxima - finish_highest)
        finish_totals = finish_totals * finish_factor + jnp.sum(fresh_weights, axis=-1)
        finish_running = finish_running * finish_factor[..., None] + jnp.einsum(
            "srht,trhd->srhd",
            fresh_weights.astype(jnp.bfloat16),
            jnp.concatenate(value_list, axis=0),
            preferred_element_type=jnp.float32,
        )
        attended = (finish_running / finish_totals[..., None]).astype(jnp.bfloat16)
        layer_attended = attended.reshape(R, local_width)
        sliced = seq_columns(layer_attended, output_weight.shape[0])
        attention_out = seq_total(
            jnp.dot(sliced, output_weight, preferred_element_type=jnp.float32)
        )
        attention_squares = feature_sums(
            jnp.sum(attention_out * attention_out, axis=1, keepdims=True)
        )
        hidden = (
            token_rows.astype(jnp.float32)
            + attention_out * inverse_rms(attention_squares[:, 0]) * attention_gain
        ).astype(jnp.bfloat16)
        hidden_cols = seq_columns(hidden, gate_weight.shape[0])
        gate_part = jnp.dot(hidden_cols, gate_weight, preferred_element_type=jnp.float32)
        up_part = jnp.dot(hidden_cols, up_weight, preferred_element_type=jnp.float32)
        hidden_units = gate_weight.shape[1]
        summed_both = seq_total(jnp.concatenate([gate_part, up_part], axis=1))
        active = (
            jax.nn.silu(summed_both[:, :hidden_units]) * summed_both[:, hidden_units:]
        ).astype(jnp.bfloat16)
        active_cols = seq_columns(active, down_weight.shape[0])
        mlp_out = seq_total(jnp.dot(active_cols, down_weight, preferred_element_type=jnp.float32))
        mlp_squares = feature_sums(jnp.sum(mlp_out * mlp_out, axis=1, keepdims=True))
        outputs.append(
            (
                hidden.astype(jnp.float32)
                + mlp_out * inverse_rms(mlp_squares[:, 0]) * feedforward_gain
            ).astype(jnp.bfloat16)
        )
    return jnp.stack(outputs, axis=0)


def solution(mesh):
    in_specs = (
        P(None, None, "mp"),
        P("seq", "mp"),
        P("seq", "mp"),
        P("seq", "mp"),
        P("seq", "mp"),
        P("seq", "mp"),
        P("seq", "mp"),
        P("seq", "mp"),
        P("mp"),
        P("mp"),
        P("mp"),
        P("mp"),
        P("seq", None, "mp"),
        P("seq", None, "mp"),
        P(),
        P("seq"),
        P("seq"),
    )
    out_specs = P(None, None, "mp")
    return jax.shard_map(local, mesh=mesh, in_specs=in_specs, out_specs=out_specs, check_vma=False)
```

profile of v0, /device:TPU:6, one launch (start us, length us, event | category | flops | bytes accessed | tf_op | source)
XLA Modules:
  0.0 1058.9 jit_solution(6257620773819369397)
XLA Ops:
  7.4 13.1 %all-gather = bf16[1,16,2048]{2,1,0:T(8,128)(2,1)S(1)} all-gather(bf16[1,16,512]{2,1,0:T(8,128)(2,1)S(1)} %get-tuple-element.1524), channel_id=2, replica_groups=mesh['seq'=32,'mp'=4] {'mp'}, dimensions={2}, use_global_device_ids=true | all-gather | bytes 81920 | tf_op jit(solution)/shard_map/all_gather | solution.py:44
  72.1 104.6 %all-reduce.18.cloned.1.call-done = (f32[16,1536]{1,0:T(8,128)}, f32[16,1536]{1,0:T(8,128)}, f32[16,1536]{1,0:T(8,128)}, f32[16,1536]{1,0:T(8,128)}) async-done(((f32[16,1536]{1,0:T(8,128)}, f32[16,1536]{1,0:T(8,128)}, f32[16,1536]{1,0:T(8,128)}, f32[16,1536]{1,0:T(8,128)}), (f32[16,1536]{1,0:T(8,128)}, f32[16,1536]{1,0:T(8,128)}, f32[16,1536]{1,0:T(8,128)}, ...) | async-done | bytes 393232 | tf_op jit(solution)/shard_map/psum | solution.py:49
  190.7 26.4 %while.139 = (s32[]{:T(128)}, f32[1,16,4]{1,2,0:T(4,128)S(1)}, f32[1,16,4]{1,2,0:T(4,128)S(1)}, f32[1,16,4,128]{3,1,2,0:T(8,128)S(1)}, s32[16]{0:T(128)S(1)}, /*...) while((s32[]{:T(128)}, f32[1,16,4]{1,2,0:T(4,128)S(1)}, ...), condition=%wide.region_70.73_spmd.clone.clone, body=%wide.region_65.72_spmd.clone.clone.sunk | while | flops 2561347 | bytes 6471395 | solution.py:186
  218.1 26.4 %while.138 = (s32[]{:T(128)}, f32[1,16,4]{1,2,0:T(4,128)S(1)}, f32[1,16,4]{1,2,0:T(4,128)S(1)}, f32[1,16,4,128]{3,1,2,0:T(8,128)S(1)}, s32[16]{0:T(128)S(1)}, /*...) while((s32[]{:T(128)}, f32[1,16,4]{1,2,0:T(4,128)S(1)}, ...), condition=%wide.region_49.52_spmd.clone.clone, body=%wide.region_44.51_spmd.clone.clone.sunk | while | flops 2561347 | bytes 6471395 | solution.py:186
  245.1 26.3 %while.137 = (s32[]{:T(128)}, f32[1,16,4]{1,2,0:T(4,128)S(1)}, f32[1,16,4]{1,2,0:T(4,128)S(1)}, f32[1,16,4,128]{3,1,2,0:T(8,128)S(1)}, s32[16]{0:T(128)S(1)}, /*...) while((s32[]{:T(128)}, f32[1,16,4]{1,2,0:T(4,128)S(1)}, ...), condition=%wide.region_28.31_spmd.clone.clone, body=%wide.region_23.30_spmd.clone.clone.sunk | while | flops 2561347 | bytes 6471395 | solution.py:186
  272.0 26.4 %while.136 = (s32[]{:T(128)}, f32[1,16,4]{1,2,0:T(4,128)S(1)}, f32[1,16,4]{1,2,0:T(4,128)S(1)}, f32[1,16,4,128]{3,1,2,0:T(8,128)S(1)}, s32[16]{0:T(128)S(1)}, /*...) while((s32[]{:T(128)}, f32[1,16,4]{1,2,0:T(4,128)S(1)}, ...), condition=%wide.region_9.12_spmd.clone.clone, body=%wide.region_4.11_spmd.clone.clone.sunk | while | flops 2561347 | bytes 6471395 | solution.py:186
  301.5 21.3 %all-gather.13 = f32[32,16,4]{1,2,0:T(4,128)S(1)} all-gather(f32[1,16,4]{1,2,0:T(4,128)S(1)} %get-tuple-element.937), channel_id=15, replica_groups=mesh['seq'=32,'mp'=4] {'seq'}, dimensions={0}, use_global_device_ids=true | all-gather | bytes 8448 | tf_op jit(solution)/shard_map/all_gather | solution.py:19
  322.8 24.2 %all-gather.14 = f32[32,16,4]{1,2,0:T(4,128)S(1)} all-gather(f32[1,16,4]{1,2,0:T(4,128)S(1)} %get-tuple-element.938), channel_id=16, replica_groups=mesh['seq'=32,'mp'=4] {'seq'}, dimensions={0}, use_global_device_ids=true | all-gather | bytes 8448 | tf_op jit(solution)/shard_map/all_gather | solution.py:19
  347.6 21.6 %all-gather.9 = f32[32,16,4]{1,2,0:T(4,128)S(1)} all-gather(f32[1,16,4]{1,2,0:T(4,128)S(1)} %get-tuple-element.931), channel_id=11, replica_groups=mesh['seq'=32,'mp'=4] {'seq'}, dimensions={0}, use_global_device_ids=true | all-gather | bytes 8448 | tf_op jit(solution)/shard_map/all_gather | solution.py:19
  369.2 24.0 %all-gather.10 = f32[32,16,4]{1,2,0:T(4,128)S(1)} all-gather(f32[1,16,4]{1,2,0:T(4,128)S(1)} %get-tuple-element.932), channel_id=12, replica_groups=mesh['seq'=32,'mp'=4] {'seq'}, dimensions={0}, use_global_device_ids=true | all-gather | bytes 8448 | tf_op jit(solution)/shard_map/all_gather | solution.py:19
  393.7 21.6 %all-gather.5 = f32[32,16,4]{1,2,0:T(4,128)S(1)} all-gather(f32[1,16,4]{1,2,0:T(4,128)S(1)} %get-tuple-element.925), channel_id=7, replica_groups=mesh['seq'=32,'mp'=4] {'seq'}, dimensions={0}, use_global_device_ids=true | all-gather | bytes 8448 | tf_op jit(solution)/shard_map/all_gather | solution.py:19
  415.3 24.0 %all-gather.6 = f32[32,16,4]{1,2,0:T(4,128)S(1)} all-gather(f32[1,16,4]{1,2,0:T(4,128)S(1)} %get-tuple-element.926), channel_id=8, replica_groups=mesh['seq'=32,'mp'=4] {'seq'}, dimensions={0}, use_global_device_ids=true | all-gather | bytes 8448 | tf_op jit(solution)/shard_map/all_gather | solution.py:19
  439.8 21.6 %all-gather.1 = f32[32,16,4]{1,2,0:T(4,128)S(1)} all-gather(f32[1,16,4]{1,2,0:T(4,128)S(1)} %get-tuple-element.919), channel_id=3, replica_groups=mesh['seq'=32,'mp'=4] {'seq'}, dimensions={0}, use_global_device_ids=true | all-gather | bytes 8448 | tf_op jit(solution)/shard_map/all_gather | solution.py:19
  461.3 24.0 %all-gather.2 = f32[32,16,4]{1,2,0:T(4,128)S(1)} all-gather(f32[1,16,4]{1,2,0:T(4,128)S(1)} %get-tuple-element.920), channel_id=4, replica_groups=mesh['seq'=32,'mp'=4] {'seq'}, dimensions={0}, use_global_device_ids=true | all-gather | bytes 8448 | tf_op jit(solution)/shard_map/all_gather | solution.py:19
  488.8 12.3 %while.135 = (s32[]{:T(128)}, f32[1,16,4]{1,2,0:T(4,128)S(1)}, f32[1,16,4]{1,2,0:T(4,128)S(1)}, f32[1,16,4,128]{3,2,1,0:T(4,128)S(1)}, f32[31,1,16,4]{2,3,1,0:T(...) while((s32[]{:T(128)}, f32[1,16,4]{1,2,0:T(4,128)S(1)}, ...), condition=%wide.region_72.75_spmd, body=%wide.region_71.74_spmd.sunk | while | flops 25026 | bytes 168809 | solution.py:22
  503.6 12.3 %while.134 = (s32[]{:T(128)}, f32[1,16,4]{1,2,0:T(4,128)S(1)}, f32[1,16,4]{1,2,0:T(4,128)S(1)}, f32[1,16,4,128]{3,2,1,0:T(4,128)S(1)}, f32[31,1,16,4]{2,3,1,0:T(...) while((s32[]{:T(128)}, f32[1,16,4]{1,2,0:T(4,128)S(1)}, ...), condition=%wide.region_51.54_spmd, body=%wide.region_50.53_spmd.sunk | while | flops 25026 | bytes 168809 | solution.py:22
  527.6 12.3 %while.133 = (s32[]{:T(128)}, f32[1,16,4]{1,2,0:T(4,128)S(1)}, f32[1,16,4]{1,2,0:T(4,128)S(1)}, f32[1,16,4,128]{3,2,1,0:T(4,128)S(1)}, f32[31,1,16,4]{2,3,1,0:T(...) while((s32[]{:T(128)}, f32[1,16,4]{1,2,0:T(4,128)S(1)}, ...), condition=%wide.region_30.33_spmd, body=%wide.region_29.32_spmd.sunk | while | flops 25026 | bytes 168809 | solution.py:22
  541.5 12.3 %all_gather.157 = bf16[16,2048]{1,0:T(8,128)(2,1)S(1)} all-gather(bf16[16,512]{1,0:T(8,128)(2,1)S(1)} %bitcast.1038), channel_id=1, replica_groups=mesh['seq'=32,'mp'=4] {'mp'}, dimensions={1}, use_global_device_ids=true | all-gather | bytes 81920 | tf_op jit(solution)/shard_map/all_gather | solution.py:44
  581.9 12.3 %while.132 = (s32[]{:T(128)}, f32[1,16,4]{1,2,0:T(4,128)S(1)}, f32[1,16,4]{1,2,0:T(4,128)S(1)}, f32[1,16,4,128]{3,2,1,0:T(4,128)S(1)}, f32[31,1,16,4]{2,3,1,0:T(...) while((s32[]{:T(128)}, f32[1,16,4]{1,2,0:T(4,128)S(1)}, ...), condition=%wide.region_11.14_spmd, body=%wide.region_10.13_spmd.sunk | while | flops 25026 | bytes 168809 | solution.py:22
  607.4 101.3 %all-reduce.14.cloned.1.call-done = (f32[16,512]{1,0:T(8,128)}, f32[16,512]{1,0:T(8,128)}, f32[16,512]{1,0:T(8,128)}, f32[16,512]{1,0:T(8,128)}) async-done(((f32[16,512]{1,0:T(8,128)}, f32[16,512]{1,0:T(8,128)}, f32[16,512]{1,0:T(8,128)}, f32[16,512]{1,0:T(8,128)}), (f32[16,512]{1,0:T(8,128)}, f32[16,512]{1,0:T(8,128)}, f32[16,512]{1,0:T(8,128)}, f32[16,512]{1,0:T(8,128)})) %all-reduce.14.cloned.1.call-update) | async-done | bytes 131088 | tf_op jit(solution)/shard_map/psum | solution.py:49
  776.3 103.1 %all-reduce.16.cloned.1.call-done = (f32[16,4096]{1,0:T(8,128)}, f32[16,4096]{1,0:T(8,128)}, f32[16,4096]{1,0:T(8,128)}, f32[16,4096]{1,0:T(8,128)}) async-done(((f32[16,4096]{1,0:T(8,128)}, f32[16,4096]{1,0:T(8,128)}, f32[16,4096]{1,0:T(8,128)}, f32[16,4096]{1,0:T(8,128)}), (f32[16,4096]{1,0:T(8,128)}, f32[16,4096]{1,0:T(8,128)}, f32[16,4096]{1,0:T(8,128)}, ...) | async-done | bytes 1048592 | tf_op jit(solution)/shard_map/psum | solution.py:49
  880.4 13.0 %all_gather.159 = bf16[16,8192]{1,0:T(8,128)(2,1)S(1)} all-gather(bf16[16,2048]{1,0:T(8,128)(2,1)S(1)} %fusion.120), channel_id=1, replica_groups=mesh['seq'=32,'mp'=4] {'mp'}, dimensions={1}, use_global_device_ids=true | all-gather | bytes 327680 | tf_op jit(solution)/shard_map/all_gather | solution.py:44
  909.2 12.3 %all_gather.139 = bf16[16,8192]{1,0:T(8,128)(2,1)S(1)} all-gather(bf16[16,2048]{1,0:T(8,128)(2,1)S(1)} %fusion.122), channel_id=1, replica_groups=mesh['seq'=32,'mp'=4] {'mp'}, dimensions={1}, use_global_device_ids=true | all-gather | bytes 327680 | tf_op jit(solution)/shard_map/all_gather | solution.py:44
  936.3 100.0 %all-reduce.12.cloned.1.call-done = (f32[16,512]{1,0:T(8,128)}, f32[16,512]{1,0:T(8,128)}, f32[16,512]{1,0:T(8,128)}, f32[16,512]{1,0:T(8,128)}) async-done(((f32[16,512]{1,0:T(8,128)}, f32[16,512]{1,0:T(8,128)}, f32[16,512]{1,0:T(8,128)}, f32[16,512]{1,0:T(8,128)}), (f32[16,512]{1,0:T(8,128)}, f32[16,512]{1,0:T(8,128)}, f32[16,512]{1,0:T(8,128)}, f32[16,512]{1,0:T(8,128)})) %all-reduce.12.cloned.1.call-update) | async-done | bytes 131088 | tf_op jit(solution)/shard_map/psum | solution.py:49
  (1501 shorter events, 397.0 us)
Async XLA Ops:
  6.5 729.2 %copy-start = (bf16[64,2048]{1,0:T(8,128)(2,1)S(1)}, bf16[64,2048]{1,0:T(8,128)(2,1)}, u32[]{:S(2)}) copy-start(bf16[64,2048]{1,0:T(8,128)(2,1)} %param.43) | copy-start | bytes 786436
  6.5 184.2 %copy-start.14 = (s32[16]{0:T(128)S(1)}, s32[16]{0:T(128)}, u32[]{:S(2)}) copy-start(s32[16]{0:T(128)} %param.51) | copy-start | bytes 196
  6.5 184.2 %copy-start.7 = (s32[16]{0:T(128)S(1)}, s32[16]{0:T(128)}, u32[]{:S(2)}) copy-start(s32[16]{0:T(128)} %param.52) | copy-start | bytes 196
  6.5 184.2 %copy-start.15 = (s32[16]{0:T(128)S(1)}, s32[16]{0:T(128)}, u32[]{:S(2)}) copy-start(s32[16]{0:T(128)} %param.53) | copy-start | bytes 196
  6.5 170.2 %all-reduce.18.cloned.1.call-start = ((), (), s32[]{:S(2)}) async-start(), calls=%async_computation.7 | async-start | bytes 786432 | tf_op jit(solution)/shard_map/psum | solution.py:49
  71.0 415.7 %all-gather.27.cloned.1.call-start = ((), (), s32[]{:S(2)}) async-start(), calls=%async_computation.3 | async-start | bytes 1081344 | tf_op jit(solution)/shard_map/all_gather | solution.py:19
  217.1 0.6 copy-start.11
  217.7 283.7 %all-gather.25.cloned.1.call-start = ((), (), s32[]{:S(2)}) async-start(), calls=%async_computation.2 | async-start | bytes 1081344 | tf_op jit(solution)/shard_map/all_gather | solution.py:19
  271.5 253.9 %all-gather.23.cloned.1.call-start = ((), (), s32[]{:S(2)}) async-start(), calls=%async_computation.1 | async-start | bytes 1081344 | tf_op jit(solution)/shard_map/all_gather | solution.py:19
  298.4 187.8 %copy-start.8 = (f32[1,16,4,128]{3,1,2,0:T(8,128)}, f32[1,16,4,128]{3,1,2,0:T(8,128)S(1)}, u32[]{:S(2)}) copy-start(f32[1,16,4,128]{3,1,2,0:T(8,128)S(1)} %get-tuple-element.921) | copy-start | bytes 98308
  461.3 42.3 %copy-start.4 = (f32[32,16,4]{1,2,0:T(4,128)}, f32[32,16,4]{1,2,0:T(4,128)S(1)}, u32[]{:S(2)}) copy-start(f32[32,16,4]{1,2,0:T(4,128)S(1)} %all-gather.1) | copy-start | bytes 24580
  485.4 18.3 %copy-start.5 = (f32[32,16,4]{1,2,0:T(4,128)}, f32[32,16,4]{1,2,0:T(4,128)S(1)}, u32[]{:S(2)}) copy-start(f32[32,16,4]{1,2,0:T(4,128)S(1)} %all-gather.2) | copy-start | bytes 24580
  485.9 94.0 %all-gather.21.cloned.1.call-start = ((), (), s32[]{:S(2)}) async-start(), calls=%async_computation | async-start | bytes 1081344 | tf_op jit(solution)/shard_map/all_gather | solution.py:19
  486.5 222.2 %all-reduce.14.cloned.1.call-start = ((), (), s32[]{:S(2)}) async-start(), calls=%async_computation.5 | async-start | bytes 262144 | tf_op jit(solution)/shard_map/psum | solution.py:49
  502.3 75.2 %copy-start.3 = (bf16[64,512]{1,0:T(8,128)(2,1)S(1)}, bf16[64,512]{1,0:T(8,128)(2,1)}, u32[]{:S(2)}) copy-start(bf16[64,512]{1,0:T(8,128)(2,1)} %param.41) | copy-start | bytes 196612
  515.9 66.0 %slice-start = ((f32[32,16,4]{1,2,0:T(4,128)}), f32[1,16,4]{1,2,0:T(4,128)S(1)}, s32[]{:S(2)}) async-start(f32[32,16,4]{1,2,0:T(4,128)} %copy-done.4), calls=%async_computation.8 | async-start | bytes 4096 | tf_op jit(solution)/shard_map/slice | solution.py:20
  515.9 66.0 %slice-start.1 = ((f32[32,16,4]{1,2,0:T(4,128)}), f32[1,16,4]{1,2,0:T(4,128)S(1)}, s32[]{:S(2)}) async-start(f32[32,16,4]{1,2,0:T(4,128)} %copy-done.5), calls=%async_computation.9 | async-start | bytes 4096 | tf_op jit(solution)/shard_map/slice | solution.py:20
  526.2 196.7 %copy-start.6 = (bf16[4,16,512]{2,1,0:T(8,128)(2,1)S(1)}, bf16[4,16,512]{2,1,0:T(8,128)(2,1)}, u32[]{:S(2)}) copy-start(bf16[4,16,512]{2,1,0:T(8,128)(2,1)} %param.37) | copy-start | bytes 196612
  526.2 196.7 %copy-start.12 = (f32[512]{0:T(512)S(1)}, f32[512]{0:T(512)}, u32[]{:S(2)}) copy-start(f32[512]{0:T(512)} %param.47) | copy-start | bytes 6148
  527.6 208.4 %copy-start.1 = (bf16[64,2048]{1,0:T(8,128)(2,1)S(1)}, bf16[64,2048]{1,0:T(8,128)(2,1)}, u32[]{:S(2)}) copy-start(bf16[64,2048]{1,0:T(8,128)(2,1)} %param.42) | copy-start | bytes 786436
  607.4 272.0 %all-reduce.16.cloned.1.call-start = ((), (), s32[]{:S(2)}) async-start(), calls=%async_computation.6 | async-start | bytes 2097152 | tf_op jit(solution)/shard_map/psum | solution.py:49
  709.5 197.2 %copy-start.2 = (bf16[256,512]{1,0:T(8,128)(2,1)S(1)}, bf16[256,512]{1,0:T(8,128)(2,1)}, u32[]{:S(2)}) copy-start(bf16[256,512]{1,0:T(8,128)(2,1)} %param.44) | copy-start | bytes 786436
  760.8 289.7 %copy-start.13 = (f32[512]{0:T(512)S(1)}, f32[512]{0:T(512)}, u32[]{:S(2)}) copy-start(f32[512]{0:T(512)} %param.48) | copy-start | bytes 6148
  776.2 260.1 %all-reduce.12.cloned.1.call-start = ((), (), s32[]{:S(2)}) async-start(), calls=%async_computation.4 | async-start | bytes 262144 | tf_op jit(solution)/shard_map/psum | solution.py:49
  (2 other events, 1.2 us)
Sparse Core Ops, SparseCore 0:
  71.1 105.5 all-reduce.17
  217.9 38.5 all-gather.26
  271.6 38.4 all-gather.24
  486.0 39.4 all-gather.22
  527.5 41.8 all-gather.20
  607.5 101.1 all-reduce.13
  776.3 102.9 all-reduce.15
  936.5 99.7 all-reduce.11
where the time goes:
time: 1060 us
  waiting for transfers between devices  419 us (40%)
  blocking collectives  408 us (38%)
  local copies, waits for them, and re-layouts  86.7 us (8%)
  other arithmetic  64.3 us (6%)
  matrix products  60.5 us (6%)
  between operations  14.4 us (1%)
    psum x4, waiting for transfers between devices, seq_total(): return lax.psum(partial_value, 'seq')  409 us
    all_gather x16, blocking collectives, seq_columns(): gathered = lax.all_gather(token_rows, 'mp', axis=1, tiled=True)  194 us
    all_gather x8, blocking collectives, combined_all(): pieces = jax.tree.map(lambda part: lax.all_gather(part, axis), value)  182 us
    psum x3, blocking collectives, feature_sums(): return lax.psum(squares, 'mp')  32 us
    dot_general x16, matrix products, fold_block(): jnp.einsum('sghd,gthd->sgth', picked, key_block, preferred_element_type=j...  25.3 us
  transfers between devices with their start and end apart: 8, of which 5 were waited for; matrix products, arithmetic and copies ran while one was open for 12% of the time, Pallas kernels for 0%

commit v1 on v0

--- a/solution.py
+++ b/solution.py
@@ -13,6 +13,19 @@
 very_low = -1e30
 exact_mode = lax.Precision.HIGHEST
 pages_per_block = 4
+
+
+def ring_gather(x, axis, dim):
+    ways = lax.axis_size(axis)
+    up = [(d, (d + 1) % ways) for d in range(ways)]
+    down = [(d, (d - 1) % ways) for d in range(ways)]
+    earlier, later = ([x], [x])
+    for _ in range(ways // 2):
+        earlier.append(lax.ppermute(earlier[-1], axis, up))
+    for _ in range((ways - 1) // 2):
+        later.append(lax.ppermute(later[-1], axis, down))
+    line = jnp.concatenate([*earlier[::-1], *later[1:]], axis=dim)
+    return jnp.roll(line, (lax.axis_index(axis) - ways // 2) * x.shape[dim], axis=dim)
 
 
 def combined_all(value, axis, join):
@@ -41,7 +54,7 @@
 
 
 def seq_columns(token_rows, width):
-    gathered = lax.all_gather(token_rows, "mp", axis=1, tiled=True)
+    gathered = ring_gather(token_rows, "mp", 1)
     return lax.dynamic_slice_in_dim(gathered, lax.axis_index("seq") * width, width, 1)
 
 

time: 1060 us -> 968 us (0.913)
  blocking collectives: 408 us -> 215 us
  starting transfers between devices: 0.51 us -> 57.9 us
  waiting for transfers between devices: 419 us -> 459 us
    all_gather x16 -> x0, blocking collectives: 194 us -> none  [seq_columns(): gathered = lax.all_gather(token_rows, 'mp', axis=1, tiled=True)]
    ppermute x0 -> x48, starting transfers between devices: none -> 57.3 us  [the longest x16 43.9 us: ring_gather(): later.append(lax.ppermute(later[-1], axis, down))]
    ppermute x0 -> x48, waiting for transfers between devices: none -> 21 us  [the longest x32 21 us: ring_gather(): earlier.append(lax.ppermute(earlier[-1], axis, up))]
    all_gather x4, waiting for transfers between devices: 9.29 us -> 30.2 us  [combined_all(): pieces = jax.tree.map(lambda part: lax.all_gather(part, axis), value)]
  transfers between devices with their start and end apart: 8 -> 56, of which waited for: 5 -> 19; matrix products, arithmetic and copies ran while one was open for 12% -> 17% of each run, Pallas kernels for 0% -> 0%
where the time goes in v1:
time: 968 us; the launch traced here: 964 us
  waiting for transfers between devices  459 us (47%)
  blocking collectives  215 us (22%)
  local copies, waits for them, and re-layouts  86.8 us (9%)
  other arithmetic  65 us (7%)
  matrix products  61.1 us (6%)
  starting transfers between devices  57.9 us (6%)
  between operations  14.6 us (2%)
    psum x4, waiting for transfers between devices, seq_total(): return lax.psum(partial_value, 'seq')  407 us
    all_gather x8, blocking collectives, combined_all(): pieces = jax.tree.map(lambda part: lax.all_gather(part, axis), value)  182 us
    ppermute x16, starting transfers between devices, ring_gather(): later.append(lax.ppermute(later[-1], axis, down))  43.9 us
    psum x3, blocking collectives, feature_sums(): return lax.psum(squares, 'mp')  32 us
    all_gather x4, waiting for transfers between devices, combined_all(): pieces = jax.tree.map(lambda part: lax.all_gather(part, axis), value)  30.2 us
    dot_general x16, matrix products, fold_block(): jnp.einsum('sghd,gthd->sgth', picked, key_block, preferred_element_type=j...  25.3 us
    dynamic_slice x16, local copies, waits for them, and re-layouts, fold_block(): lax.dynamic_slice_in_dim(value_cache, first_page, pages_per_block, 0)  21.1 us
    ppermute x32, waiting for transfers between devices, ring_gather(): earlier.append(lax.ppermute(earlier[-1], axis, up))  21 us
  transfers between devices with their start and end apart: 56, of which 19 were waited for; matrix products, arithmetic and copies ran while one was open for 17% of the time, Pallas kernels for 0%

profile of v1, /device:TPU:6, one launch (start us, length us, event | category | flops | bytes accessed | tf_op | source)
XLA Modules:
  0.0 964.4 jit_solution(4742902132112001146)
XLA Ops:
  42.9 106.3 %all-reduce.18.cloned.1.call-done = (f32[16,1536]{1,0:T(8,128)}, f32[16,1536]{1,0:T(8,128)}, f32[16,1536]{1,0:T(8,128)}, f32[16,1536]{1,0:T(8,128)}) async-done(((f32[16,1536]{1,0:T(8,128)}, f32[16,1536]{1,0:T(8,128)}, f32[16,1536]{1,0:T(8,128)}, f32[16,1536]{1,0:T(8,128)}), (f32[16,1536]{1,0:T(8,128)}, f32[16,1536]{1,0:T(8,128)}, f32[16,1536]{1,0:T(8,128)}, ...) | async-done | bytes 393232 | tf_op jit(solution)/shard_map/psum | solution.py:62
  151.2 10.7 %all-reduce.6 = (f32[16,2]{0,1:T(2,128)S(1)}, f32[16,2]{0,1:T(2,128)S(1)}, f32[16,2]{0,1:T(2,128)S(1)}, f32[16,2]{0,1:T(2,128)S(1)}) all-reduce(f32[16,2]{0,1:T(2,128)S(1)} %pad_maximum_fusion.19, f32[16,2]{0,1:T(2,128)S(1)} %pad_maximum_fusion.18, f32[16,2]{0,1:T(2,128)S(1)} %pad_maximum_fusion.17, ...), channel_id=1, replica_groups=mesh['seq'=32,'mp'=4] {'mp'}, use_global_device_ids=true, to_apply=%region_64.69 | all-reduce | flops 128 | bytes 1024 | tf_op jit(solution)/shard_map/psum | solution.py:66
  163.3 26.4 %while.139 = (s32[]{:T(128)}, f32[1,16,4]{1,2,0:T(4,128)S(1)}, f32[1,16,4]{1,2,0:T(4,128)S(1)}, f32[1,16,4,128]{3,1,2,0:T(8,128)S(1)}, s32[16]{0:T(128)S(1)}, /*...) while((s32[]{:T(128)}, f32[1,16,4]{1,2,0:T(4,128)S(1)}, ...), condition=%wide.region_70.75_spmd.clone.clone, body=%wide.region_65.74_spmd.clone.clone.sunk | while | flops 2561347 | bytes 6471395 | solution.py:199
  190.6 26.4 %while.138 = (s32[]{:T(128)}, f32[1,16,4]{1,2,0:T(4,128)S(1)}, f32[1,16,4]{1,2,0:T(4,128)S(1)}, f32[1,16,4,128]{3,1,2,0:T(8,128)S(1)}, s32[16]{0:T(128)S(1)}, /*...) while((s32[]{:T(128)}, f32[1,16,4]{1,2,0:T(4,128)S(1)}, ...), condition=%wide.region_49.54_spmd.clone.clone, body=%wide.region_44.53_spmd.clone.clone.sunk | while | flops 2561347 | bytes 6471395 | solution.py:199
  217.6 26.3 %while.137 = (s32[]{:T(128)}, f32[1,16,4]{1,2,0:T(4,128)S(1)}, f32[1,16,4]{1,2,0:T(4,128)S(1)}, f32[1,16,4,128]{3,1,2,0:T(8,128)S(1)}, s32[16]{0:T(128)S(1)}, /*...) while((s32[]{:T(128)}, f32[1,16,4]{1,2,0:T(4,128)S(1)}, ...), condition=%wide.region_28.33_spmd.clone.clone, body=%wide.region_23.32_spmd.clone.clone.sunk | while | flops 2561347 | bytes 6471395 | solution.py:199
  244.6 26.4 %while.136 = (s32[]{:T(128)}, f32[1,16,4]{1,2,0:T(4,128)S(1)}, f32[1,16,4]{1,2,0:T(4,128)S(1)}, f32[1,16,4,128]{3,1,2,0:T(8,128)S(1)}, s32[16]{0:T(128)S(1)}, /*...) while((s32[]{:T(128)}, f32[1,16,4]{1,2,0:T(4,128)S(1)}, ...), condition=%wide.region_9.13_spmd.clone.clone, body=%wide.region_4.12_spmd.clone.clone.sunk | while | flops 2561347 | bytes 6471395 | solution.py:199
  274.0 21.3 %all-gather.9 = f32[32,16,4]{1,2,0:T(4,128)S(1)} all-gather(f32[1,16,4]{1,2,0:T(4,128)S(1)} %get-tuple-element.939), channel_id=11, replica_groups=mesh['seq'=32,'mp'=4] {'seq'}, dimensions={0}, use_global_device_ids=true | all-gather | bytes 8448 | tf_op jit(solution)/shard_map/all_gather | solution.py:32
  295.4 24.4 %all-gather.10 = f32[32,16,4]{1,2,0:T(4,128)S(1)} all-gather(f32[1,16,4]{1,2,0:T(4,128)S(1)} %get-tuple-element.940), channel_id=12, replica_groups=mesh['seq'=32,'mp'=4] {'seq'}, dimensions={0}, use_global_device_ids=true | all-gather | bytes 8448 | tf_op jit(solution)/shard_map/all_gather | solution.py:32
  320.4 21.6 %all-gather.6 = f32[32,16,4]{1,2,0:T(4,128)S(1)} all-gather(f32[1,16,4]{1,2,0:T(4,128)S(1)} %get-tuple-element.933), channel_id=8, replica_groups=mesh['seq'=32,'mp'=4] {'seq'}, dimensions={0}, use_global_device_ids=true | all-gather | bytes 8448 | tf_op jit(solution)/shard_map/all_gather | solution.py:32
  342.0 24.0 %all-gather.7 = f32[32,16,4]{1,2,0:T(4,128)S(1)} all-gather(f32[1,16,4]{1,2,0:T(4,128)S(1)} %get-tuple-element.934), channel_id=9, replica_groups=mesh['seq'=32,'mp'=4] {'seq'}, dimensions={0}, use_global_device_ids=true | all-gather | bytes 8448 | tf_op jit(solution)/shard_map/all_gather | solution.py:32
  366.5 21.6 %all-gather.3 = f32[32,16,4]{1,2,0:T(4,128)S(1)} all-gather(f32[1,16,4]{1,2,0:T(4,128)S(1)} %get-tuple-element.927), channel_id=5, replica_groups=mesh['seq'=32,'mp'=4] {'seq'}, dimensions={0}, use_global_device_ids=true | all-gather | bytes 8448 | tf_op jit(solution)/shard_map/all_gather | solution.py:32
  388.0 24.0 %all-gather.4 = f32[32,16,4]{1,2,0:T(4,128)S(1)} all-gather(f32[1,16,4]{1,2,0:T(4,128)S(1)} %get-tuple-element.928), channel_id=6, replica_groups=mesh['seq'=32,'mp'=4] {'seq'}, dimensions={0}, use_global_device_ids=true | all-gather | bytes 8448 | tf_op jit(solution)/shard_map/all_gather | solution.py:32
  412.5 21.6 %all-gather = f32[32,16,4]{1,2,0:T(4,128)S(1)} all-gather(f32[1,16,4]{1,2,0:T(4,128)S(1)} %get-tuple-element.921), channel_id=2, replica_groups=mesh['seq'=32,'mp'=4] {'seq'}, dimensions={0}, use_global_device_ids=true | all-gather | bytes 8448 | tf_op jit(solution)/shard_map/all_gather | solution.py:32
  434.1 24.0 %all-gather.1 = f32[32,16,4]{1,2,0:T(4,128)S(1)} all-gather(f32[1,16,4]{1,2,0:T(4,128)S(1)} %get-tuple-element.922), channel_id=3, replica_groups=mesh['seq'=32,'mp'=4] {'seq'}, dimensions={0}, use_global_device_ids=true | all-gather | bytes 8448 | tf_op jit(solution)/shard_map/all_gather | solution.py:32
  461.3 12.3 %while.135 = (s32[]{:T(128)}, f32[1,16,4]{1,2,0:T(4,128)S(1)}, f32[1,16,4]{1,2,0:T(4,128)S(1)}, f32[1,16,4,128]{3,2,1,0:T(4,128)S(1)}, f32[31,1,16,4]{2,3,1,0:T(...) while((s32[]{:T(128)}, f32[1,16,4]{1,2,0:T(4,128)S(1)}, ...), condition=%wide.region_72.77_spmd, body=%wide.region_71.76_spmd.sunk | while | flops 25026 | bytes 168809 | solution.py:35
  478.6 12.3 %while.134 = (s32[]{:T(128)}, f32[1,16,4]{1,2,0:T(4,128)S(1)}, f32[1,16,4]{1,2,0:T(4,128)S(1)}, f32[1,16,4,128]{3,2,1,0:T(4,128)S(1)}, f32[31,1,16,4]{2,3,1,0:T(...) while((s32[]{:T(128)}, f32[1,16,4]{1,2,0:T(4,128)S(1)}, ...), condition=%wide.region_51.56_spmd, body=%wide.region_50.55_spmd.sunk | while | flops 25026 | bytes 168809 | solution.py:35
  500.4 12.3 %while.133 = (s32[]{:T(128)}, f32[1,16,4]{1,2,0:T(4,128)S(1)}, f32[1,16,4]{1,2,0:T(4,128)S(1)}, f32[1,16,4,128]{3,2,1,0:T(4,128)S(1)}, f32[31,1,16,4]{2,3,1,0:T(...) while((s32[]{:T(128)}, f32[1,16,4]{1,2,0:T(4,128)S(1)}, ...), condition=%wide.region_30.35_spmd, body=%wide.region_29.34_spmd.sunk | while | flops 25026 | bytes 168809 | solution.py:35
  516.4 25.8 %all-gather.17.cloned.1.call-done = f32[32,16,4,128]{3,1,2,0:T(8,128)} async-done(((f32[1,16,4,128]{3,1,2,0:T(8,128)}), f32[32,16,4,128]{3,1,2,0:T(8,128)}) %all-gather.17.cloned.1.call-update) | async-done | bytes 1048592 | tf_op jit(solution)/shard_map/all_gather | solution.py:32
  544.3 12.3 %while.132 = (s32[]{:T(128)}, f32[1,16,4]{1,2,0:T(4,128)S(1)}, f32[1,16,4]{1,2,0:T(4,128)S(1)}, f32[1,16,4,128]{3,2,1,0:T(4,128)S(1)}, f32[31,1,16,4]{2,3,1,0:T(...) while((s32[]{:T(128)}, f32[1,16,4]{1,2,0:T(4,128)S(1)}, ...), condition=%wide.region_11.15_spmd, body=%wide.region_10.14_spmd.sunk | while | flops 25026 | bytes 168809 | solution.py:35
  572.9 99.7 %all-reduce.14.cloned.1.call-done = (f32[16,512]{1,0:T(8,128)}, f32[16,512]{1,0:T(8,128)}, f32[16,512]{1,0:T(8,128)}, f32[16,512]{1,0:T(8,128)}) async-done(((f32[16,512]{1,0:T(8,128)}, f32[16,512]{1,0:T(8,128)}, f32[16,512]{1,0:T(8,128)}, f32[16,512]{1,0:T(8,128)}), (f32[16,512]{1,0:T(8,128)}, f32[16,512]{1,0:T(8,128)}, f32[16,512]{1,0:T(8,128)}, f32[16,512]{1,0:T(8,128)})) %all-reduce.14.cloned.1.call-update) | async-done | bytes 131088 | tf_op jit(solution)/shard_map/psum | solution.py:62
  676.1 10.7 %all-reduce.5 = (f32[16,1]{0,1:T(1,128)S(1)}, f32[16,1]{0,1:T(1,128)S(1)}, f32[16,1]{0,1:T(1,128)S(1)}, f32[16,1]{0,1:T(1,128)S(1)}) all-reduce(f32[16,1]{0,1:T(1,128)S(1)} %bitcast.1045, f32[16,1]{0,1:T(1,128)S(1)} %bitcast.1046, f32[16,1]{0,1:T(1,128)S(1)} %bitcast.1047, ...), channel_id=1, replica_groups=mesh['seq'=32,'mp'=4] {'mp'}, use_global_device_ids=true, to_apply=%region_77.82 | all-reduce | flops 64 | bytes 512 | tf_op jit(solution)/shard_map/psum | solution.py:66
  710.4 102.7 %all-reduce.16.cloned.1.call-done = (f32[16,4096]{1,0:T(8,128)}, f32[16,4096]{1,0:T(8,128)}, f32[16,4096]{1,0:T(8,128)}, f32[16,4096]{1,0:T(8,128)}) async-done(((f32[16,4096]{1,0:T(8,128)}, f32[16,4096]{1,0:T(8,128)}, f32[16,4096]{1,0:T(8,128)}, f32[16,4096]{1,0:T(8,128)}), (f32[16,4096]{1,0:T(8,128)}, f32[16,4096]{1,0:T(8,128)}, f32[16,4096]{1,0:T(8,128)}, ...) | async-done | bytes 1048592 | tf_op jit(solution)/shard_map/psum | solution.py:62
  843.1 98.7 %all-reduce.12.cloned.1.call-done = (f32[16,512]{1,0:T(8,128)}, f32[16,512]{1,0:T(8,128)}, f32[16,512]{1,0:T(8,128)}, f32[16,512]{1,0:T(8,128)}) async-done(((f32[16,512]{1,0:T(8,128)}, f32[16,512]{1,0:T(8,128)}, f32[16,512]{1,0:T(8,128)}, f32[16,512]{1,0:T(8,128)}), (f32[16,512]{1,0:T(8,128)}, f32[16,512]{1,0:T(8,128)}, f32[16,512]{1,0:T(8,128)}, f32[16,512]{1,0:T(8,128)})) %all-reduce.12.cloned.1.call-update) | async-done | bytes 131088 | tf_op jit(solution)/shard_map/psum | solution.py:62
  945.3 10.7 %all-reduce.4 = (f32[16,1]{0,1:T(1,128)S(1)}, f32[16,1]{0,1:T(1,128)S(1)}, f32[16,1]{0,1:T(1,128)S(1)}, f32[16,1]{0,1:T(1,128)S(1)}) all-reduce(f32[16,1]{0,1:T(1,128)S(1)} %bitcast.1048, f32[16,1]{0,1:T(1,128)S(1)} %bitcast.1049, f32[16,1]{0,1:T(1,128)S(1)} %bitcast.1050, ...), channel_id=1, replica_groups=mesh['seq'=32,'mp'=4] {'mp'}, use_global_device_ids=true, to_apply=%region_81.86 | all-reduce | flops 64 | bytes 512 | tf_op jit(solution)/shard_map/psum | solution.py:66
  (1585 shorter events, 296.5 us)
Async XLA Ops:
  6.5 142.7 %all-reduce.18.cloned.1.call-start = ((), (), s32[]{:S(2)}) async-start(), calls=%async_computation.7 | async-start | bytes 786432 | tf_op jit(solution)/shard_map/psum | solution.py:62
  7.4 11.5 %collective-permute-start.2 = (bf16[16,512]{1,0:T(8,128)(2,1)S(1)}, bf16[16,512]{1,0:T(8,128)(2,1)S(1)}, u32[]{:S(2)}, u32[]{:S(2)}) collective-permute-start(bf16[16,512]{1,0:T(8,128)(2,1)S(1)} %get-tuple-element.1526), channel_id=1, source_target_pairs={{0,3},{1,0},{2,1},{3,2},{4,7},{5,4},{6,5},{7,6},{8,11},{9,8},{10,9... | collective-permute-start | bytes 49160 | tf_op jit(solution)/shard_map/ppermute | solution.py:26
  11.4 14.3 %collective-permute-start.38 = (bf16[16,512]{1,0:T(8,128)(2,1)S(1)}, bf16[16,512]{1,0:T(8,128)(2,1)S(1)}, u32[]{:S(2)}, u32[]{:S(2)}) collective-permute-start(bf16[16,512]{1,0:T(8,128)(2,1)S(1)} %get-tuple-element.1527), channel_id=1, source_target_pairs={{0,3},{1,0},{2,1},{3,2},{4,7},{5,4},{6,5},{7,6},{8,11},{9,8},{10,9... | collective-permute-start | bytes 49160 | tf_op jit(solution)/shard_map/ppermute | solution.py:26
  14.7 18.4 %collective-permute-start.26 = (bf16[16,512]{1,0:T(8,128)(2,1)S(1)}, bf16[16,512]{1,0:T(8,128)(2,1)S(1)}, u32[]{:S(2)}, u32[]{:S(2)}) collective-permute-start(bf16[16,512]{1,0:T(8,128)(2,1)S(1)} %get-tuple-element.1528), channel_id=1, source_target_pairs={{0,3},{1,0},{2,1},{3,2},{4,7},{5,4},{6,5},{7,6},{8,11},{9,8},{10,9... | collective-permute-start | bytes 49160 | tf_op jit(solution)/shard_map/ppermute | solution.py:26
  18.9 10.1 %collective-permute-start.24 = (bf16[16,512]{1,0:T(8,128)(2,1)S(1)}, bf16[16,512]{1,0:T(8,128)(2,1)S(1)}, u32[]{:S(2)}, u32[]{:S(2)}) collective-permute-start(bf16[16,512]{1,0:T(8,128)(2,1)S(1)} %get-tuple-element.1528), channel_id=1, source_target_pairs={{0,1},{1,2},{2,3},{3,0},{4,5},{5,6},{6,7},{7,4},{8,9},{9,10},{10,1... | collective-permute-start | bytes 49160 | tf_op jit(solution)/shard_map/ppermute | solution.py:24
  25.8 11.2 %collective-permute-start.14 = (bf16[16,512]{1,0:T(8,128)(2,1)S(1)}, bf16[16,512]{1,0:T(8,128)(2,1)S(1)}, u32[]{:S(2)}, u32[]{:S(2)}) collective-permute-start(bf16[16,512]{1,0:T(8,128)(2,1)S(1)} %get-tuple-element.1525), channel_id=1, source_target_pairs={{0,3},{1,0},{2,1},{3,2},{4,7},{5,4},{6,5},{7,6},{8,11},{9,8},{10,9... | collective-permute-start | bytes 49160 | tf_op jit(solution)/shard_map/ppermute | solution.py:26
  42.6 416.6 %all-gather.23.cloned.1.call-start = ((), (), s32[]{:S(2)}) async-start(), calls=%async_computation.3 | async-start | bytes 1081344 | tf_op jit(solution)/shard_map/all_gather | solution.py:32
  190.3 286.2 %all-gather.21.cloned.1.call-start = ((), (), s32[]{:S(2)}) async-start(), calls=%async_computation.2 | async-start | bytes 1081344 | tf_op jit(solution)/shard_map/all_gather | solution.py:32
  244.0 254.2 %all-gather.19.cloned.1.call-start = ((), (), s32[]{:S(2)}) async-start(), calls=%async_computation.1 | async-start | bytes 1081344 | tf_op jit(solution)/shard_map/all_gather | solution.py:32
  458.6 83.6 %all-gather.17.cloned.1.call-start = ((), (), s32[]{:S(2)}) async-start(), calls=%async_computation | async-start | bytes 1081344 | tf_op jit(solution)/shard_map/all_gather | solution.py:32
  459.2 213.4 %all-reduce.14.cloned.1.call-start = ((), (), s32[]{:S(2)}) async-start(), calls=%async_computation.5 | async-start | bytes 262144 | tf_op jit(solution)/shard_map/psum | solution.py:62
  474.4 84.1 %collective-permute-start.41 = (bf16[16,512]{1,0:T(8,128)(2,1)S(1)}, bf16[16,512]{1,0:T(8,128)(2,1)S(1)}, u32[]{:S(2)}, u32[]{:S(2)}) collective-permute-start(bf16[16,512]{1,0:T(8,128)(2,1)S(1)} %bitcast.1026), channel_id=1, source_target_pairs={{0,3},{1,0},{2,1},{3,2},{4,7},{5,4},{6,5},{7,6},{8,11},{9,8},{10,9... | collective-permute-start | bytes 49160 | tf_op jit(solution)/shard_map/ppermute | solution.py:26
  474.5 82.4 %collective-permute-start.39 = (bf16[16,512]{1,0:T(8,128)(2,1)S(1)}, bf16[16,512]{1,0:T(8,128)(2,1)S(1)}, u32[]{:S(2)}, u32[]{:S(2)}) collective-permute-start(bf16[16,512]{1,0:T(8,128)(2,1)S(1)} %bitcast.1027), channel_id=1, source_target_pairs={{0,1},{1,2},{2,3},{3,0},{4,5},{5,6},{6,7},{7,4},{8,9},{9,10},{10,1... | collective-permute-start | bytes 49160 | tf_op jit(solution)/shard_map/ppermute | solution.py:24
  491.6 71.4 %collective-permute-start.29 = (bf16[16,512]{1,0:T(8,128)(2,1)S(1)}, bf16[16,512]{1,0:T(8,128)(2,1)S(1)}, u32[]{:S(2)}, u32[]{:S(2)}) collective-permute-start(bf16[16,512]{1,0:T(8,128)(2,1)S(1)} %bitcast.1029), channel_id=1, source_target_pairs={{0,3},{1,0},{2,1},{3,2},{4,7},{5,4},{6,5},{7,6},{8,11},{9,8},{10,9... | collective-permute-start | bytes 49160 | tf_op jit(solution)/shard_map/ppermute | solution.py:26
  493.0 67.2 %collective-permute-start.27 = (bf16[16,512]{1,0:T(8,128)(2,1)S(1)}, bf16[16,512]{1,0:T(8,128)(2,1)S(1)}, u32[]{:S(2)}, u32[]{:S(2)}) collective-permute-start(bf16[16,512]{1,0:T(8,128)(2,1)S(1)} %bitcast.1030), channel_id=1, source_target_pairs={{0,1},{1,2},{2,3},{3,0},{4,5},{5,6},{6,7},{7,4},{8,9},{9,10},{10,1... | collective-permute-start | bytes 49160 | tf_op jit(solution)/shard_map/ppermute | solution.py:24
  513.4 54.2 %collective-permute-start.17 = (bf16[16,512]{1,0:T(8,128)(2,1)S(1)}, bf16[16,512]{1,0:T(8,128)(2,1)S(1)}, u32[]{:S(2)}, u32[]{:S(2)}) collective-permute-start(bf16[16,512]{1,0:T(8,128)(2,1)S(1)} %bitcast.1032), channel_id=1, source_target_pairs={{0,3},{1,0},{2,1},{3,2},{4,7},{5,4},{6,5},{7,6},{8,11},{9,8},{10,9... | collective-permute-start | bytes 49160 | tf_op jit(solution)/shard_map/ppermute | solution.py:26
  572.6 240.5 %all-reduce.16.cloned.1.call-start = ((), (), s32[]{:S(2)}) async-start(), calls=%async_computation.6 | async-start | bytes 2097152 | tf_op jit(solution)/shard_map/psum | solution.py:62
  696.0 9.7 %collective-permute-start.20 = (bf16[16,512]{1,0:T(8,128)(2,1)S(1)}, bf16[16,512]{1,0:T(8,128)(2,1)S(1)}, u32[]{:S(2)}, u32[]{:S(2)}) collective-permute-start(bf16[16,512]{1,0:T(8,128)(2,1)S(1)} %get-tuple-element.1522), channel_id=1, source_target_pairs={{0,3},{1,0},{2,1},{3,2},{4,7},{5,4},{6,5},{7,6},{8,11},{9,8},{10,9... | collective-permute-start | bytes 49160 | tf_op jit(solution)/shard_map/ppermute | solution.py:26
  699.5 9.4 collective-permute-start.8
  710.3 231.5 %all-reduce.12.cloned.1.call-start = ((), (), s32[]{:S(2)}) async-start(), calls=%async_computation.4 | async-start | bytes 262144 | tf_op jit(solution)/shard_map/psum | solution.py:62
  814.1 12.7 %collective-permute-start.47 = (bf16[16,2048]{1,0:T(8,128)(2,1)S(1)}, bf16[16,2048]{1,0:T(8,128)(2,1)S(1)}, u32[]{:S(2)}, u32[]{:S(2)}) collective-permute-start(bf16[16,2048]{1,0:T(8,128)(2,1)S(1)} %fusion.120), channel_id=1, source_target_pairs={{0,3},{1,0},{2,1},{3,2},{4,7},{5,4},{6,5},{7,6},{8,11},{9,8},{10,9... | collective-permute-start | bytes 196616 | tf_op jit(solution)/shard_map/ppermute | solution.py:26
  818.1 14.4 %collective-permute-start.35 = (bf16[16,2048]{1,0:T(8,128)(2,1)S(1)}, bf16[16,2048]{1,0:T(8,128)(2,1)S(1)}, u32[]{:S(2)}, u32[]{:S(2)}) collective-permute-start(bf16[16,2048]{1,0:T(8,128)(2,1)S(1)} %fusion.121), channel_id=1, source_target_pairs={{0,3},{1,0},{2,1},{3,2},{4,7},{5,4},{6,5},{7,6},{8,11},{9,8},{10,9... | collective-permute-start | bytes 196616 | tf_op jit(solution)/shard_map/ppermute | solution.py:26
  822.4 15.6 %collective-permute-start.23 = (bf16[16,2048]{1,0:T(8,128)(2,1)S(1)}, bf16[16,2048]{1,0:T(8,128)(2,1)S(1)}, u32[]{:S(2)}, u32[]{:S(2)}) collective-permute-start(bf16[16,2048]{1,0:T(8,128)(2,1)S(1)} %fusion.122), channel_id=1, source_target_pairs={{0,3},{1,0},{2,1},{3,2},{4,7},{5,4},{6,5},{7,6},{8,11},{9,8},{10,9... | collective-permute-start | bytes 196616 | tf_op jit(solution)/shard_map/ppermute | solution.py:26
  832.5 9.6 collective-permute-start.11
  (50 other events, 2769.2 us)
Sparse Core Ops, SparseCore 0:
  42.8 106.4 all-reduce.17
  190.4 38.5 all-gather.22
  244.2 38.3 all-gather.20
  458.7 39.4 all-gather.18
  500.3 41.8 all-gather.16
  572.7 99.7 all-reduce.13
  710.4 102.5 all-reduce.15
  843.2 98.5 all-reduce.11
